TPU v7x, 512 devices: a whole 4x8x8 slice. The times are simulated.
512 devices in a mesh: req: 64 (over y, z), tp: 8 (over x, core).
Axes of the slice: x: 4, y: 8, z: 8, core: 2. Of those that a mesh axis runs over, the one named last changes fastest.
Arguments:
- hidden_in: bfloat16 [64, 512, 1024], P(None, 'req', 'tp'), may hold values from -64 to 64
- cache_keys: bfloat16 [64, 512, 1024], P('req', None, 'tp'), may hold values from -250 to 250
- cache_values: bfloat16 [64, 512, 1024], P('req', None, 'tp'), may hold values from -6 to 6
- cache_lengths: int32 [64], replicated, may hold values from 32 to 512, as said below
- owner_order: int32 [64], replicated, may hold values from 0 to 63, as said below
- request_slot: int32 [64], replicated, may hold values from 0 to 63, as said below
- proj_weight: bfloat16 [3, 1024, 1024], P(None, None, 'tp'), may hold values from -0.0625 to 0.0625
- proj_bias: bfloat16 [3, 1024], P(None, 'tp'), may hold values from -1.5 to 1.5
- output_weight: bfloat16 [1024, 1024], P('tp'), may hold values from -0.75 to 0.75
- output_bias: bfloat16 [1024], replicated, may hold values from -2.5 to 2.5
- norm_gains: bfloat16 [2, 1024], replicated, may hold values from 0.5 to 1.5
- norm_biases: bfloat16 [2, 1024], replicated, may hold values from -2.5 to 2.5
- widen_weight: bfloat16 [1024, 4096], P(None, 'tp'), may hold values from -0.1875 to 0.1875
- widen_bias: bfloat16 [4096], P('tp'), may hold values from -2.5 to 2.5
- narrow_weight: bfloat16 [4096, 1024], P('tp'), may hold values from -0.09375 to 0.09375
- narrow_bias: bfloat16 [1024], replicated, may hold values from -2.5 to 2.5
Outputs:
- hidden_out: bfloat16 [64, 512, 1024], P(None, 'req', 'tp')
- new_cache: bfloat16 [2, 64, 512, 1024], P(None, 'req', None, 'tp')
Inputs may be any that keep to these rules, and one draw needn't show every extreme that they name: owner_order is a permutation of the requests; owner slot s lies on index s // 1 of req. request_slot[owner_order[s]] = s for every slot s. `cache_lengths`: given in request order; the longest is exactly 512.
All inputs are finite; a program needn't handle non-finite values.
Results may differ from a plain program's by a relative error of at most 0.014.
Values may be sent and summed in bfloat16 or wider, within the bound.
No kernel may reach another device: no remote copies, remote signals or barrier semaphores. Data moves between devices by JAX's collectives and lax.ppermute only.
A program may use at most 64 MiB of HBM per device.

v0:
```python
import jax
import jax.numpy as jnp
from jax import lax
from jax.sharding import PartitionSpec as P

HD = 64


def layer_norm(values, scale_row, shift_row):
    average = jnp.mean(values, axis=-1, keepdims=True)
    centred = values - average
    spread = jnp.mean(centred * centred, axis=-1, keepdims=True)
    return centred * lax.rsqrt(spread + 1e-05) * scale_row.astype(jnp.float32) + shift_row.astype(
        jnp.float32
    )


def split_heads(rows_block):
    return rows_block.reshape(rows_block.shape[0], -1, HD)


def block_scores(query_heads, keys_block, allowed):
    scores = jnp.einsum(
        "thd,shd->hts", query_heads, split_heads(keys_block), preferred_element_type=jnp.float32
    )
    return jnp.where(allowed[None], scores, -jnp.inf)


def to_rows(factor):
    return jnp.transpose(factor, (1, 0, 2))


def slot_attention(fields):
    query_rows, key_rows, value_rows, slot_keys, slot_values, length = fields
    fresh_len = query_rows.shape[0]
    block_len = min(512, slot_keys.shape[0])
    block_count = slot_keys.shape[0] // block_len
    query_heads = split_heads(query_rows)
    self_mask = jnp.arange(fresh_len)[:, None] >= jnp.arange(fresh_len)[None, :]
    self_scores = block_scores(query_heads, key_rows, self_mask)
    row_top = jnp.max(self_scores, axis=2, keepdims=True)
    raised = jnp.exp(self_scores - row_top)
    row_total = jnp.sum(raised, axis=2, keepdims=True)
    context = jnp.einsum(
        "hts,shd->thd",
        raised.astype(jnp.bfloat16),
        split_heads(value_rows),
        preferred_element_type=jnp.float32,
    )
    positions = jnp.arange(block_len)

    def one_block(number, carry):
        old_top, old_total, running = carry
        begin_at = number * block_len
        allowed = jnp.broadcast_to((begin_at + positions < length)[None, :], (fresh_len, block_len))
        scores = block_scores(query_heads, slot_keys, allowed)
        new_top = jnp.maximum(old_top, jnp.max(scores, axis=2, keepdims=True))
        factor = jnp.exp(old_top - new_top)
        block_raised = jnp.exp(scores - new_top)
        new_total = old_total * factor + jnp.sum(block_raised, axis=2, keepdims=True)
        added = jnp.einsum(
            "hts,shd->thd",
            block_raised.astype(jnp.bfloat16),
            split_heads(slot_values),
            preferred_element_type=jnp.float32,
        )
        return (new_top, new_total, running * to_rows(factor) + added)

    row_top, row_total, context = lax.fori_loop(
        0, block_count, one_block, (row_top, row_total, context)
    )
    context = context / to_rows(row_total)
    return context.reshape(fresh_len, -1).astype(jnp.bfloat16)


def widen_rows(normed, widen_weight, widen_bias):
    widened = jnp.dot(normed, widen_weight, preferred_element_type=jnp.float32) + widen_bias.astype(
        jnp.float32
    )
    return jax.nn.gelu(widened, approximate=False).astype(jnp.bfloat16)


def on_device(
    hidden_in,
    cache_keys,
    cache_values,
    cache_lengths,
    owner_order,
    request_slot,
    proj_weight,
    proj_bias,
    output_weight,
    output_bias,
    norm_gains,
    norm_biases,
    widen_weight,
    widen_bias,
    narrow_weight,
    narrow_bias,
):
    slot_count = cache_keys.shape[0]
    fresh_len = hidden_in.shape[1] * lax.axis_size("req")
    owned_slots = lax.dynamic_slice_in_dim(
        owner_order, lax.axis_index("req") * slot_count, slot_count
    )
    lengths = jnp.take(cache_lengths, owned_slots)
    gathered = lax.all_gather(hidden_in, "tp", axis=2, tiled=True)
    token_rows = lax.all_to_all(
        jnp.take(gathered, owner_order, axis=0), "req", split_axis=0, concat_axis=1, tiled=True
    )
    flat_rows = token_rows.reshape(slot_count * fresh_len, -1)
    projected = (
        jnp.einsum("td,cdf->ctf", flat_rows, proj_weight, preferred_element_type=jnp.float32)
        + proj_bias.astype(jnp.float32)[:, None, :]
    )
    query_rows = (
        (projected[0] * HD ** (-0.5)).astype(jnp.bfloat16).reshape(slot_count, fresh_len, -1)
    )
    key_rows = projected[1].astype(jnp.bfloat16).reshape(slot_count, fresh_len, -1)
    value_rows = projected[2].astype(jnp.bfloat16).reshape(slot_count, fresh_len, -1)
    new_cache = jnp.stack([key_rows, value_rows], axis=0)
    context = lax.map(
        slot_attention, (query_rows, key_rows, value_rows, cache_keys, cache_values, lengths)
    )
    context = context.reshape(slot_count * fresh_len, -1)
    tp_count = lax.axis_size("tp")
    attended = lax.psum(
        jnp.dot(context, output_weight, preferred_element_type=jnp.float32).astype(jnp.bfloat16),
        "tp",
    ).astype(jnp.float32)
    normed = layer_norm(
        flat_rows.astype(jnp.float32) + attended + output_bias.astype(jnp.float32),
        norm_gains[0],
        norm_biases[0],
    ).astype(jnp.bfloat16)
    activated = widen_rows(normed, widen_weight, widen_bias)
    fed_total = lax.psum(
        jnp.dot(activated, narrow_weight, preferred_element_type=jnp.float32).astype(jnp.bfloat16),
        "tp",
    ).astype(jnp.float32)
    updated = layer_norm(
        normed.astype(jnp.float32) + fed_total + narrow_bias.astype(jnp.float32),
        norm_gains[1],
        norm_biases[1],
    ).astype(jnp.bfloat16)
    column_count = updated.shape[1] // tp_count
    updated = lax.dynamic_slice_in_dim(
        updated, lax.axis_index("tp") * column_count, column_count, 1
    )
    returned = lax.all_to_all(
        updated.reshape(slot_count, fresh_len, -1), "req", split_axis=1, concat_axis=0, tiled=True
    )
    hidden_out = jnp.take(returned, request_slot, axis=0)
    return (hidden_out, new_cache)


def solution(mesh):
    in_specs = (
        P(None, "req", "tp"),
        P("req", None, "tp"),
        P("req", None, "tp"),
        P(),
        P(),
        P(),
        P(None, None, "tp"),
        P(None, "tp"),
        P("tp", None),
        P(),
        P(),
        P(),
        P(None, "tp"),
        P("tp"),
        P("tp", None),
        P(),
    )
    out_specs = (P(None, "req", "tp"), P(None, "req", None, "tp"))
    return jax.shard_map(
        on_device, mesh=mesh, in_specs=in_specs, out_specs=out_specs, check_vma=False
    )
```

profile of v0, /device:TPU:8, one launch (start us, length us, event | category | flops | bytes accessed | tf_op | source)
XLA Modules:
  0.0 283.8 jit_solution(11562906684038777593)
XLA Ops:
  7.2 0.7 all-gather.2.cloned.1.call-update
  7.9 0.7 compare_select_fusion
  8.6 0.7 compare_and_fusion
  9.2 34.1 %all-gather.2.cloned.1.call-done = bf16[64,8,1024]{2,1,0:T(8,128)(2,1)} async-done(((bf16[64,8,128]{2,1,0:T(8,128)(2,1)}), bf16[64,8,1024]{2,1,0:T(8,128)(2,1)}) %all-gather.2.cloned.1.call-update) | async-done | bytes 1048592 | tf_op jit(solution)/shard_map/all_gather | solution.py:107
  43.3 1.8 gather_fusion
  45.2 1.1 broadcast_select_fusion
  46.3 13.5 %all-to-all-start = ((bf16[64,8,1024]{2,1,0:T(8,128)(2,1)}), bf16[64,8,1024]{2,1,0:T(8,128)(2,1)S(1)}, u32[]{:S(2)}, u32[]{:S(2)}) async-start(bf16[64,8,1024]{2,1,0:T(8,128)(2,1)} %broadcast_select_fusion), calls=%async_computation | async-start | bytes 2097152 | tf_op jit(solution)/shard_map/all_to_all | solution.py:108
  60.0 0.6 dynamic_slice.20
  62.6 1.4 copy.36
  64.0 0.8 copy.38
  64.8 0.7 dynamic-slice.5
  66.2 23.3 %all-to-all-done = bf16[64,8,1024]{2,1,0:T(8,128)(2,1)S(1)} async-done(((bf16[64,8,1024]{2,1,0:T(8,128)(2,1)}), bf16[64,8,1024]{2,1,0:T(8,128)(2,1)S(1)}, u32[]{:S(2)}, u32[]{:S(2)}) %all-to-all-start) | async-done | bytes 1048608 | tf_op jit(solution)/shard_map/all_to_all | solution.py:108
  89.5 0.6 fusion.16
  90.9 0.6 select_reduce_fusion.1
  91.5 0.6 convolution_bitcast_fusion
  92.1 0.9 fusion.2
  93.0 0.7 fusion.10
  93.9 1.5 convolution_convert_fusion
  95.8 68.0 %all-reduce.3.cloned.1.call-done = bf16[512,1024]{1,0:T(8,128)(2,1)} async-done(((bf16[512,1024]{1,0:T(8,128)(2,1)}), bf16[512,1024]{1,0:T(8,128)(2,1)}) %all-reduce.3.cloned.1.call-update) | async-done | bytes 1048592 | tf_op jit(solution)/shard_map/psum | solution.py:127
  163.8 1.7 fusion.6
  166.1 0.6 add_convert_fusion
  166.7 5.6 %convolution_convert_fusion.1 = bf16[512,1024]{1,0:T(8,128)(2,1)} fusion(bf16[512,1024]{1,0:T(8,128)(2,1)S(1)} %copy-done, bf16[512,1024]{1,0:T(8,128)(2,1)S(1)} %add_convert_fusion, bf16[1024,512]{1,0:T(8,128)(2,1)} %param.28, f32[512]{0:T(512)S(1)} %convert_element_type.122), kind=kOutput, calls=%fused_computation.20 | convolution fusion | flops 1091567616 | bytes 4196352 | tf_op jit(solution)/shard_map/dot_general | solution.py:138
  172.6 72.7 %all-reduce.5.cloned.1.call-done = bf16[512,1024]{1,0:T(8,128)(2,1)} async-done(((bf16[512,1024]{1,0:T(8,128)(2,1)}), bf16[512,1024]{1,0:T(8,128)(2,1)}) %all-reduce.5.cloned.1.call-update) | async-done | bytes 1048592 | tf_op jit(solution)/shard_map/psum | solution.py:137
  245.3 1.7 fusion.1
  247.0 0.6 multiply_reduce_fusion
  248.5 1.4 reduce
  249.9 0.7 reshape.238
  250.6 13.4 %all-to-all-start.1 = ((bf16[64,2,512]{2,1,0:T(2,128)(2,1)}), bf16[64,2,512]{2,1,0:T(2,128)(2,1)S(1)}, u32[]{:S(2)}, u32[]{:S(2)}) async-start(bf16[64,2,512]{2,1,0:T(2,128)(2,1)} %reshape.238), calls=%async_computation.1 | async-start | bytes 262144 | tf_op jit(solution)/shard_map/all_to_all | solution.py:150
  264.0 0.8 copy.42
  264.9 10.8 %all-to-all-done.1 = bf16[64,2,512]{2,1,0:T(2,128)(2,1)S(1)} async-done(((bf16[64,2,512]{2,1,0:T(2,128)(2,1)}), bf16[64,2,512]{2,1,0:T(2,128)(2,1)S(1)}, u32[]{:S(2)}, u32[]{:S(2)}) %all-to-all-start.1) | async-done | bytes 131104 | tf_op jit(solution)/shard_map/all_to_all | solution.py:150
  275.8 0.6 gather_fusion.1
  276.5 0.8 broadcast_select_fusion.1
  (69 shorter events, 3.4 us)
Async XLA Ops:
  7.2 159.5 %copy-start = (bf16[512,1024]{1,0:T(8,128)(2,1)S(1)}, bf16[512,1024]{1,0:T(8,128)(2,1)}, u32[]{:S(2)}) copy-start(bf16[512,1024]{1,0:T(8,128)(2,1)} %param.30) | copy-start | bytes 3145732
  7.2 36.1 %all-gather.2.cloned.1.call-start = ((), (), s32[]{:S(2)}) async-start(), calls=%async_computation.2 | async-start | bytes 1179648 | tf_op jit(solution)/shard_map/all_gather | solution.py:107
  45.1 14.7 %copy-start.5 = (bf16[1,512,128]{2,1,0:T(8,128)(2,1)S(1)}, bf16[1,512,128]{2,1,0:T(8,128)(2,1)}, u32[]{:S(2)}) copy-start(bf16[1,512,128]{2,1,0:T(8,128)(2,1)} %param.18) | copy-start | bytes 393220
  45.2 14.9 %copy-start.13 = (s32[64]{0:T(128)S(1)}, s32[64]{0:T(128)}, u32[]{:S(2)}) copy-start(s32[64]{0:T(128)} %param.20) | copy-start | bytes 772
  46.3 17.7 %copy-start.11 = (bf16[3,128]{1,0:T(4,128)(2,1)S(1)}, bf16[3,128]{1,0:T(4,128)(2,1)}, u32[]{:S(2)}) copy-start(bf16[3,128]{1,0:T(4,128)(2,1)} %param.23) | copy-start | bytes 2308
  46.3 17.7 %copy-start.6 = (bf16[1,512,128]{2,1,0:T(8,128)(2,1)S(1)}, bf16[1,512,128]{2,1,0:T(8,128)(2,1)}, u32[]{:S(2)}) copy-start(bf16[1,512,128]{2,1,0:T(8,128)(2,1)} %param.17) | copy-start | bytes 393220
  46.3 18.5 %copy-start.14 = (s32[64]{0:T(128)S(1)}, s32[64]{0:T(128)}, u32[]{:S(2)}) copy-start(s32[64]{0:T(128)} %param.19) | copy-start | bytes 772
  46.3 43.2 %all-to-all-start = ((bf16[64,8,1024]{2,1,0:T(8,128)(2,1)}), bf16[64,8,1024]{2,1,0:T(8,128)(2,1)S(1)}, u32[]{:S(2)}, u32[]{:S(2)}) async-start(bf16[64,8,1024]{2,1,0:T(8,128)(2,1)} %broadcast_select_fusion), calls=%async_computation | async-start | bytes 2097152 | tf_op jit(solution)/shard_map/all_to_all | solution.py:108
  59.8 103.9 %all-reduce.3.cloned.1.call-start = ((), (), s32[]{:S(2)}) async-start(), calls=%async_computation.3 | async-start | bytes 2097152 | tf_op jit(solution)/shard_map/psum | solution.py:127
  89.5 0.9 copy-start.3
  93.0 1.0 copy-start.4
  93.7 2.0 copy-start.9
  93.7 2.0 copy-start.12
  93.7 2.0 copy-start.7
  93.7 2.0 copy-start.8
  95.4 149.8 %all-reduce.5.cloned.1.call-start = ((), (), s32[]{:S(2)}) async-start(), calls=%async_computation.4 | async-start | bytes 2097152 | tf_op jit(solution)/shard_map/psum | solution.py:137
  163.8 1.7 copy-start.1
  166.7 5.7 %copy-start.10 = (bf16[1024]{0:T(1024)(128)(2,1)S(1)}, bf16[1024]{0:T(1024)(128)(2,1)}, u32[]{:S(2)}) copy-start(bf16[1024]{0:T(1024)(128)(2,1)} %param.31) | copy-start | bytes 6148
  166.7 5.9 %copy-start.15 = (s32[64]{0:T(128)S(1)}, s32[64]{0:T(128)}, u32[]{:S(2)}) copy-start(s32[64]{0:T(128)} %param.21) | copy-start | bytes 772
  245.3 1.7 copy-start.2
  250.6 25.1 %all-to-all-start.1 = ((bf16[64,2,512]{2,1,0:T(2,128)(2,1)}), bf16[64,2,512]{2,1,0:T(2,128)(2,1)S(1)}, u32[]{:S(2)}, u32[]{:S(2)}) async-start(bf16[64,2,512]{2,1,0:T(2,128)(2,1)} %reshape.238), calls=%async_computation.1 | async-start | bytes 262144 | tf_op jit(solution)/shard_map/all_to_all | solution.py:150
Sparse Core Ops, SparseCore 0:
  10.1 33.1 all-gather.1
  95.6 68.1 all-reduce.2
  172.5 72.6 all-reduce.4
where the time goes:
time: 284 us
  waiting for transfers between devices  210 us (74%)
  starting transfers between devices  27.2 us (10%)
  between operations  16.8 us (6%)
  other arithmetic  11.2 us (4%)
  matrix products  10 us (4%)
  local copies, waits for them, and re-layouts  8.95 us (3%)
    psum x1, waiting for transfers between devices, on_device(): lax.psum(jnp.dot(activated, narrow_weight, preferred_element_type=jnp.flo...  72.7 us
    psum x1, waiting for transfers between devices, on_device(): lax.psum(jnp.dot(context, output_weight, preferred_element_type=jnp.float...  68 us
    all_gather x1, waiting for transfers between devices, on_device(): gathered = lax.all_gather(hidden_in, 'tp', axis=2, tiled=True)  34.1 us
    all_to_all x1, waiting for transfers between devices, on_device(): lax.all_to_all(jnp.take(gathered, owner_order, axis=0), 'req', split_axis...  23.3 us
    all_to_all x1, starting transfers between devices, on_device(): lax.all_to_all(jnp.take(gathered, owner_order, axis=0), 'req', split_axis...  13.5 us
    all_to_all x1, starting transfers between devices, on_device(): lax.all_to_all(updated.reshape(slot_count, fresh_len, -1), 'req', split_a...  13.4 us
    all_to_all x1, waiting for transfers between devices, on_device(): lax.all_to_all(updated.reshape(slot_count, fresh_len, -1), 'req', split_a...  10.8 us
  transfers between devices with their start and end apart: 5, of which 5 were waited for; matrix products, arithmetic and copies ran while one was open for 2% of the time, Pallas kernels for 0%

commit v1 on v0

--- a/solution.py
+++ b/solution.py
@@ -134,9 +134,14 @@
         norm_biases[0],
     ).astype(jnp.bfloat16)
     activated = widen_rows(normed, widen_weight, widen_bias)
-    fed_total = lax.psum(
-        jnp.dot(activated, narrow_weight, preferred_element_type=jnp.float32).astype(jnp.bfloat16),
-        "tp",
+    fed_total = jnp.sum(
+        lax.all_gather(
+            jnp.dot(activated, narrow_weight, preferred_element_type=jnp.float32).astype(
+                jnp.bfloat16
+            ),
+            "tp",
+        ),
+        axis=0,
     ).astype(jnp.float32)
     updated = layer_norm(
         normed.astype(jnp.float32) + fed_total + narrow_bias.astype(jnp.float32),

time: 284 us -> 271 us (0.954)
  the two profiles are of different devices: /device:TPU:8 before, /device:TPU:1 now
where the time goes in v1:
time: 271 us
  waiting for transfers between devices  193 us (71%)
  starting transfers between devices  26.5 us (10%)
  between operations  16.7 us (6%)
  other arithmetic  15.6 us (6%)
  matrix products  10.1 us (4%)
  local copies, waits for them, and re-layouts  8.86 us (3%)
    psum x1, waiting for transfers between devices, on_device(): lax.psum(jnp.dot(context, output_weight, preferred_element_type=jnp.float...  69.1 us
    all_gather x1, waiting for transfers between devices, on_device(): lax.all_gather(jnp.dot(activated, narrow_weight, preferred_element_type=j...  56.3 us
    all_gather x1, waiting for transfers between devices, on_device(): gathered = lax.all_gather(hidden_in, 'tp', axis=2, tiled=True)  35.4 us
    all_to_all x1, waiting for transfers between devices, on_device(): lax.all_to_all(jnp.take(gathered, owner_order, axis=0), 'req', split_axis...  21 us
    all_to_all x1, starting transfers between devices, on_device(): lax.all_to_all(jnp.take(gathered, owner_order, axis=0), 'req', split_axis...  13.1 us
    all_to_all x1, starting transfers between devices, on_device(): lax.all_to_all(updated.reshape(slot_count, fresh_len, -1), 'req', split_a...  13 us
    all_to_all x1, waiting for transfers between devices, on_device(): lax.all_to_all(updated.reshape(slot_count, fresh_len, -1), 'req', split_a...  10.6 us
    dot_general x1, matrix products, on_device(): jnp.dot(activated, narrow_weight, preferred_element_type=jnp.float32)  5.68 us
  transfers between devices with their start and end apart: 5, of which 5 were waited for; matrix products, arithmetic and copies ran while one was open for 2% of the time, Pallas kernels for 0%

profile of v1, /device:TPU:1, one launch (start us, length us, event | category | flops | bytes accessed | tf_op | source)
XLA Modules:
  0.0 270.7 jit_solution(16115705989915387815)
XLA Ops:
  7.2 0.7 all-gather.4.cloned.1.call-update
  7.9 0.7 compare_select_fusion
  8.6 0.7 compare_and_fusion
  9.2 35.4 %all-gather.4.cloned.1.call-done = bf16[64,8,1024]{2,1,0:T(8,128)(2,1)} async-done(((bf16[64,8,128]{2,1,0:T(8,128)(2,1)}), bf16[64,8,1024]{2,1,0:T(8,128)(2,1)}) %all-gather.4.cloned.1.call-update) | async-done | bytes 1048592 | tf_op jit(solution)/shard_map/all_gather | solution.py:107
  44.6 1.8 gather_fusion
  46.5 1.1 broadcast_select_fusion
  47.6 13.1 %all-to-all-start = ((bf16[64,8,1024]{2,1,0:T(8,128)(2,1)}), bf16[64,8,1024]{2,1,0:T(8,128)(2,1)S(1)}, u32[]{:S(2)}, u32[]{:S(2)}) async-start(bf16[64,8,1024]{2,1,0:T(8,128)(2,1)} %broadcast_select_fusion), calls=%async_computation | async-start | bytes 2097152 | tf_op jit(solution)/shard_map/all_to_all | solution.py:108
  60.8 0.6 dynamic_slice.20
  63.4 1.4 copy.36
  64.8 0.8 copy.38
  67.0 21.0 %all-to-all-done = bf16[64,8,1024]{2,1,0:T(8,128)(2,1)S(1)} async-done(((bf16[64,8,1024]{2,1,0:T(8,128)(2,1)}), bf16[64,8,1024]{2,1,0:T(8,128)(2,1)S(1)}, u32[]{:S(2)}, u32[]{:S(2)}) %all-to-all-start) | async-done | bytes 1048608 | tf_op jit(solution)/shard_map/all_to_all | solution.py:108
  87.9 0.6 fusion.16
  89.3 0.6 select_reduce_fusion.1
  89.9 0.9 fusion.2
  90.8 0.6 convolution_bitcast_fusion
  91.4 0.7 fusion.10
  92.3 1.5 convolution_convert_fusion
  94.2 69.1 %all-reduce.2.cloned.1.call-done = bf16[512,1024]{1,0:T(8,128)(2,1)} async-done(((bf16[512,1024]{1,0:T(8,128)(2,1)}), bf16[512,1024]{1,0:T(8,128)(2,1)}) %all-reduce.2.cloned.1.call-update) | async-done | bytes 1048592 | tf_op jit(solution)/shard_map/psum | solution.py:127
  163.3 1.7 fusion.6
  165.0 0.6 multiply_reduce_fusion.1
  165.6 0.6 add_convert_fusion
  166.2 5.7 %convolution_convert_fusion.1 = bf16[512,1024]{1,0:T(8,128)(2,1)} fusion(bf16[512,1024]{1,0:T(8,128)(2,1)S(1)} %copy-done, bf16[512,1024]{1,0:T(8,128)(2,1)S(1)} %add_convert_fusion, bf16[1024,512]{1,0:T(8,128)(2,1)} %param.28, f32[512]{0:T(512)S(1)} %convert_element_type.124), kind=kOutput, calls=%fused_computation.20 | convolution fusion | flops 1091567616 | bytes 4196352 | tf_op jit(solution)/shard_map/dot_general | solution.py:139
  172.1 56.3 %all-gather.6.cloned.1.call-done = bf16[4096,1024]{1,0:T(8,128)(2,1)} async-done(((bf16[512,1024]{1,0:T(8,128)(2,1)}), bf16[4096,1024]{1,0:T(8,128)(2,1)}) %all-gather.6.cloned.1.call-update) | async-done | bytes 8388624 | tf_op jit(solution)/shard_map/all_gather | solution.py:138
  228.4 5.7 %reduce_sum.79 = bf16[512,1024]{1,0:T(8,128)(2,1)S(1)} reduce(bf16[8,512,1024]{2,1,0:T(8,128)(2,1)} %bitcast.88, bf16[]{:T(256)} %constant.161.clone.1), dimensions={0}, to_apply=%region_7.8 | reduce | flops 3670016 | bytes 9437186 | tf_op jit(solution)/shard_map/reduce_sum | solution.py:137
  234.5 0.6 multiply_reduce_fusion
  235.9 1.4 reduce.1
  237.4 0.7 reshape.239
  238.1 13.0 %all-to-all-start.1 = ((bf16[64,2,512]{2,1,0:T(2,128)(2,1)}), bf16[64,2,512]{2,1,0:T(2,128)(2,1)S(1)}, u32[]{:S(2)}, u32[]{:S(2)}) async-start(bf16[64,2,512]{2,1,0:T(2,128)(2,1)} %reshape.239), calls=%async_computation.1 | async-start | bytes 262144 | tf_op jit(solution)/shard_map/all_to_all | solution.py:155
  251.1 0.8 copy.42
  252.0 10.6 %all-to-all-done.1 = bf16[64,2,512]{2,1,0:T(2,128)(2,1)S(1)} async-done(((bf16[64,2,512]{2,1,0:T(2,128)(2,1)}), bf16[64,2,512]{2,1,0:T(2,128)(2,1)S(1)}, u32[]{:S(2)}, u32[]{:S(2)}) %all-to-all-start.1) | async-done | bytes 131104 | tf_op jit(solution)/shard_map/all_to_all | solution.py:155
  262.7 0.6 gather_fusion.1
  263.3 0.8 broadcast_select_fusion.1
  (68 shorter events, 3.8 us)
Async XLA Ops:
  7.2 159.0 %copy-start = (bf16[512,1024]{1,0:T(8,128)(2,1)S(1)}, bf16[512,1024]{1,0:T(8,128)(2,1)}, u32[]{:S(2)}) copy-start(bf16[512,1024]{1,0:T(8,128)(2,1)} %param.30) | copy-start | bytes 3145732
  7.2 37.4 %all-gather.4.cloned.1.call-start = ((), (), s32[]{:S(2)}) async-start(), calls=%async_computation.2 | async-start | bytes 1179648 | tf_op jit(solution)/shard_map/all_gather | solution.py:107
  46.4 14.4 %copy-start.12 = (s32[64]{0:T(128)S(1)}, s32[64]{0:T(128)}, u32[]{:S(2)}) copy-start(s32[64]{0:T(128)} %param.20) | copy-start | bytes 772
  47.6 17.2 %copy-start.10 = (bf16[3,128]{1,0:T(4,128)(2,1)S(1)}, bf16[3,128]{1,0:T(4,128)(2,1)}, u32[]{:S(2)}) copy-start(bf16[3,128]{1,0:T(4,128)(2,1)} %param.23) | copy-start | bytes 2308
  47.6 17.2 %copy-start.4 = (bf16[1,512,128]{2,1,0:T(8,128)(2,1)S(1)}, bf16[1,512,128]{2,1,0:T(8,128)(2,1)}, u32[]{:S(2)}) copy-start(bf16[1,512,128]{2,1,0:T(8,128)(2,1)} %param.17) | copy-start | bytes 393220
  47.6 18.0 %copy-start.5 = (bf16[1,512,128]{2,1,0:T(8,128)(2,1)S(1)}, bf16[1,512,128]{2,1,0:T(8,128)(2,1)}, u32[]{:S(2)}) copy-start(bf16[1,512,128]{2,1,0:T(8,128)(2,1)} %param.18) | copy-start | bytes 393220
  47.6 18.1 %copy-start.13 = (s32[64]{0:T(128)S(1)}, s32[64]{0:T(128)}, u32[]{:S(2)}) copy-start(s32[64]{0:T(128)} %param.19) | copy-start | bytes 772
  47.6 40.3 %all-to-all-start = ((bf16[64,8,1024]{2,1,0:T(8,128)(2,1)}), bf16[64,8,1024]{2,1,0:T(8,128)(2,1)S(1)}, u32[]{:S(2)}, u32[]{:S(2)}) async-start(bf16[64,8,1024]{2,1,0:T(8,128)(2,1)} %broadcast_select_fusion), calls=%async_computation | async-start | bytes 2097152 | tf_op jit(solution)/shard_map/all_to_all | solution.py:108
  60.8 102.5 %all-reduce.2.cloned.1.call-start = ((), (), s32[]{:S(2)}) async-start(), calls=%async_computation.3 | async-start | bytes 2097152 | tf_op jit(solution)/shard_map/psum | solution.py:127
  87.9 0.9 copy-start.2
  91.4 1.0 copy-start.3
  92.1 2.0 copy-start.8
  92.1 2.0 copy-start.11
  92.1 2.0 copy-start.6
  92.1 2.0 copy-start.7
  93.8 134.6 %all-gather.6.cloned.1.call-start = ((), (), s32[]{:S(2)}) async-start(), calls=%async_computation.4 | async-start | bytes 9437184 | tf_op jit(solution)/shard_map/all_gather | solution.py:138
  163.3 1.7 copy-start.1
  166.2 5.7 %copy-start.9 = (bf16[1024]{0:T(1024)(128)(2,1)S(1)}, bf16[1024]{0:T(1024)(128)(2,1)}, u32[]{:S(2)}) copy-start(bf16[1024]{0:T(1024)(128)(2,1)} %param.31) | copy-start | bytes 6148
  166.2 5.9 %copy-start.14 = (s32[64]{0:T(128)S(1)}, s32[64]{0:T(128)}, u32[]{:S(2)}) copy-start(s32[64]{0:T(128)} %param.21) | copy-start | bytes 772
  238.1 24.5 %all-to-all-start.1 = ((bf16[64,2,512]{2,1,0:T(2,128)(2,1)}), bf16[64,2,512]{2,1,0:T(2,128)(2,1)S(1)}, u32[]{:S(2)}, u32[]{:S(2)}) async-start(bf16[64,2,512]{2,1,0:T(2,128)(2,1)} %reshape.239), calls=%async_computation.1 | async-start | bytes 262144 | tf_op jit(solution)/shard_map/all_to_all | solution.py:155
Sparse Core Ops, SparseCore 0:
  10.1 34.4 all-gather.3
  94.0 69.2 all-reduce.1
  172.1 56.2 all-gather.5
